TPU v7x, 256 devices: a whole 4x4x8 slice. The times are simulated.
256 devices in a mesh: space: 16 (over x_hi, z), chan: 8 (over y, core), dp: 2 (over x_lo).
Axes of the slice: x: 4 (x_hi: 2, x_lo: 2; x = x_hi * 2 + x_lo), y: 4, z: 8, core: 2. Of those that a mesh axis runs over, the one named last changes fastest.
Arguments:
- inputs: bfloat16 [2, 32, 8, 128, 512], P('dp', 'space', None, 'chan'), may hold values from -6 to 6
- cotangent: bfloat16 [2, 32, 8, 128, 512], P('dp', 'space', None, 'chan'), may hold values from -6 to 6
- weight: bfloat16 [27, 128, 128], P(None, 'chan'), may hold values from -0.109375 to 0.109375
Outputs:
- input_grad: bfloat16 [2, 32, 8, 128, 512], P('dp', 'space', None, 'chan')
- weight_grad: float32 [27, 128, 128], P(None, 'chan')
All inputs are finite; a program needn't handle non-finite values.
Results may differ from a plain program's by a relative error of at most 0.001.
Values may be sent and summed in bfloat16 or wider, within the bound.
No kernel may reach another device: no remote copies, remote signals or barrier semaphores. Data moves between devices by JAX's collectives and lax.ppermute only.
A program may use at most 64 MiB of HBM per device.

v0:
```python
import math
import jax
import jax.numpy as jnp
from jax import lax
from jax.sharding import PartitionSpec as P


def from_behind(value, axis, steps):
    count = lax.axis_size(axis)
    initial, last = (max(0, -steps), min(count, count - steps))
    return lax.ppermute(value, axis, [(source, source + steps) for source in range(initial, last)])


def exchange_sum(value, axis, distance):
    count = lax.axis_size(axis)
    return value + lax.ppermute(value, axis, [(i, i ^ distance) for i in range(count)])


def butterfly_sum(value):
    value = exchange_sum(value, "dp", 1)
    for distance in (1, 8, 2, 4):
        value = exchange_sum(value, "space", distance)
    return value


def shift_cells(block, step_z, step_y):
    zero = jnp.zeros((), block.dtype)
    config = ((0, 0, 0), (0, 0, 0), (step_z, -step_z, 0), (0, 0, 0), (step_y, -step_y, 0))
    return lax.pad(block, zero, config)


def local(inputs, cotangent, weight):
    samples, planes, depth, channels, width = inputs.shape
    outputs = weight.shape[2]
    gathered = lax.all_gather(cotangent, "chan", axis=3, tiled=True)
    lower_plane = from_behind(gathered[:, -1:], "space", 1)
    upper_plane = from_behind(gathered[:, :1], "space", -1)
    stacked = jnp.concatenate(
        [shift_cells(inputs, -step_z, -step_y) for step_z in (-1, 0, 1) for step_y in (-1, 0, 1)],
        axis=3,
    )
    accum = jnp.zeros(inputs.shape, jnp.float32)
    groups = []
    for step_x in (-1, 0, 1):
        if step_x == 1:
            slab = jnp.concatenate([lower_plane, gathered[:, : planes - 1]], axis=1)
        elif step_x == -1:
            slab = jnp.concatenate([gathered[:, 1:], upper_plane], axis=1)
        else:
            slab = gathered
        first = 9 * (step_x + 1)
        groups.append(
            jnp.einsum("bxzky,bxzcy->kc", stacked, slab, preferred_element_type=jnp.float32)
        )
        for step_y in (-1, 0, 1):
            kernel = weight[first + step_y + 1 : first + 9 : 3].reshape(3 * channels, outputs)
            product = jnp.einsum(
                "bxzcy,kc->bxzky", slab, kernel, preferred_element_type=jnp.float32
            )
            for place, step_z in enumerate((-1, 0, 1)):
                part = product[:, :, :, place * channels : (place + 1) * channels]
                accum = accum + shift_cells(part, step_z, step_y)
    input_grad = accum.astype(jnp.bfloat16)
    local_grad = jnp.concatenate(groups, axis=0).reshape(27, channels, outputs)
    count = samples * lax.axis_size("dp") * planes * lax.axis_size("space") * depth * width
    scale = 1.0 / math.sqrt(count)
    weight_grad = butterfly_sum(local_grad) * scale
    return (input_grad, weight_grad)


def solution(mesh):
    placed = (
        P("dp", "space", None, "chan", None),
        P("dp", "space", None, "chan", None),
        P(None, "chan", None),
    )
    return jax.shard_map(
        local,
        mesh=mesh,
        in_specs=placed,
        out_specs=(P("dp", "space", None, "chan", None), P(None, "chan", None)),
        check_vma=False,
    )
```

profile of v0, /device:TPU:4, one launch (start us, length us, event | category | flops | bytes accessed | tf_op | source)
XLA Modules:
  0.0 135.7 jit_solution(2542420532690271903)
XLA Ops:
  7.2 0.0 copy-start.1
  7.2 0.0 all-gather.2.cloned.1.call-start
  7.2 0.7 all-gather.2.cloned.1.call-update
  7.9 1.1 fusion.64
  9.0 0.0 copy-start.2
  9.0 1.0 fusion.60
  10.0 1.1 fusion.65
  11.1 1.1 fusion.62
  12.2 0.0 copy-done.1
  12.2 0.1 fusion.63
  12.4 0.1 fusion.66
  12.5 0.1 fusion.67
  12.7 0.0 copy-done.2
  12.7 28.0 %all-gather.2.cloned.1.call-done = bf16[1,2,8,128,512]{4,3,2,1,0:T(8,128)(2,1)} async-done(((bf16[1,2,8,16,512]{4,3,2,1,0:T(8,128)(2,1)}), bf16[1,2,8,128,512]{4,3,2,1,0:T(8,128)(2,1)}) %all-gather.2.cloned.1.call-update) | async-done | bytes 2097168 | tf_op jit(solution)/shard_map/all_gather | solution.py:35
  40.7 0.0 copy-start
  40.7 1.9 %fusion.68 = (bf16[1,1,8,128,512]{4,3,2,1,0:T(8,128)(2,1)S(1)}, bf16[1,1,8,128,512]{4,3,2,1,0:T(8,128)(2,1)S(1)}) fusion(bf16[1,2,8,128,512]{4,3,2,1,0:T(8,128)(2,1)} %all-gather.2.cloned.1.call-done), kind=kLoop, calls=%fused_computation.97 | loop fusion | bytes 4194304 | tf_op jit(solution)/shard_map/slice | solution.py:48
  42.6 5.2 %collective-permute-start = (bf16[1,1,8,128,512]{4,3,2,1,0:T(8,128)(2,1)S(1)}, bf16[1,1,8,128,512]{4,3,2,1,0:T(8,128)(2,1)S(1)}, u32[]{:S(2)}, u32[]{:S(2)}) collective-permute-start(bf16[1,1,8,128,512]{4,3,2,1,0:T(8,128)(2,1)S(1)} %get-tuple-element.3), channel_id=1, source_target_pairs={{16,0},{32,16},{48,32},{64,48},{80,64},{96,80},{112,96},{128,112},... | collective-permute-start | bytes 3145736 | tf_op jit(solution)/shard_map/ppermute | solution.py:11
  47.8 1.9 %collective-permute-start.1 = (bf16[1,1,8,128,512]{4,3,2,1,0:T(8,128)(2,1)S(1)}, bf16[1,1,8,128,512]{4,3,2,1,0:T(8,128)(2,1)S(1)}, u32[]{:S(2)}, u32[]{:S(2)}) collective-permute-start(bf16[1,1,8,128,512]{4,3,2,1,0:T(8,128)(2,1)S(1)} %get-tuple-element.2), channel_id=1, source_target_pairs={{0,16},{16,32},{32,48},{48,64},{64,80},{80,96},{96,112},{112,128},... | collective-permute-start | bytes 3145736 | tf_op jit(solution)/shard_map/ppermute | solution.py:11
  49.7 0.0 copy-done
  49.7 0.4 fusion.19
  50.1 0.1 fusion.74
  50.3 0.4 fusion.16
  50.7 0.4 fusion.13
  51.1 0.4 fusion.72
  51.5 0.8 fusion.25
  52.3 18.3 %collective-permute-done = bf16[1,1,8,128,512]{4,3,2,1,0:T(8,128)(2,1)S(1)} collective-permute-done((bf16[1,1,8,128,512]{4,3,2,1,0:T(8,128)(2,1)S(1)}, bf16[1,1,8,128,512]{4,3,2,1,0:T(8,128)(2,1)S(1)}, u32[]{:S(2)}, u32[]{:S(2)}) %collective-permute-start) | collective-permute-done | bytes 1048608 | tf_op jit(solution)/shard_map/ppermute | solution.py:11
  70.6 0.8 fusion.22
  71.3 7.1 %collective-permute-done.1 = bf16[1,1,8,128,512]{4,3,2,1,0:T(8,128)(2,1)S(1)} collective-permute-done((bf16[1,1,8,128,512]{4,3,2,1,0:T(8,128)(2,1)S(1)}, bf16[1,1,8,128,512]{4,3,2,1,0:T(8,128)(2,1)S(1)}, u32[]{:S(2)}, u32[]{:S(2)}) %collective-permute-start.1) | collective-permute-done | bytes 1048608 | tf_op jit(solution)/shard_map/ppermute | solution.py:11
  78.4 0.8 fusion.30
  79.2 2.2 %collective-permute-start.2 = (f32[27,16,128]{2,1,0:T(8,128)S(1)}, f32[27,16,128]{2,1,0:T(8,128)S(1)}, u32[]{:S(2)}, u32[]{:S(2)}) collective-permute-start(f32[27,16,128]{2,1,0:T(8,128)S(1)} %bitcast.157), channel_id=1, source_target_pairs={{0,1},{1,0},{2,3},{3,2},{4,5},{5,4},{6,7},{7,6},{8,9},{9,8},{10,11... | collective-permute-start | bytes 663560 | tf_op jit(solution)/shard_map/ppermute | solution.py:16
  81.4 0.4 convolution_bitcast_fusion.4
  81.8 0.4 convolution_bitcast_fusion.5
  82.2 0.4 fusion.69
  82.6 0.4 convolution_bitcast_fusion.1
  83.1 0.4 convolution_bitcast_fusion.2
  83.5 2.5 %collective-permute-done.2 = f32[27,16,128]{2,1,0:T(8,128)S(1)} collective-permute-done((f32[27,16,128]{2,1,0:T(8,128)S(1)}, f32[27,16,128]{2,1,0:T(8,128)S(1)}, u32[]{:S(2)}, u32[]{:S(2)}) %collective-permute-start.2) | collective-permute-done | bytes 221216 | tf_op jit(solution)/shard_map/ppermute | solution.py:16
  86.0 0.1 collective-permute-start.3
  86.1 0.4 fusion.75
  86.5 0.4 convolution_bitcast_fusion.3
  87.0 5.1 %collective-permute-done.3 = f32[27,16,128]{2,1,0:T(8,128)S(1)} collective-permute-done((f32[27,16,128]{2,1,0:T(8,128)S(1)}, f32[27,16,128]{2,1,0:T(8,128)S(1)}, u32[]{:S(2)}, u32[]{:S(2)}) %collective-permute-start.3) | collective-permute-done | bytes 221216 | tf_op jit(solution)/shard_map/ppermute | solution.py:16
  92.1 0.1 collective-permute-start.4
  92.2 0.1 fusion.71
  92.3 0.4 convolution_bitcast_fusion
  92.7 6.9 %collective-permute-done.4 = f32[27,16,128]{2,1,0:T(8,128)S(1)} collective-permute-done((f32[27,16,128]{2,1,0:T(8,128)S(1)}, f32[27,16,128]{2,1,0:T(8,128)S(1)}, u32[]{:S(2)}, u32[]{:S(2)}) %collective-permute-start.4) | collective-permute-done | bytes 221216 | tf_op jit(solution)/shard_map/ppermute | solution.py:16
  99.6 0.1 collective-permute-start.5
  99.7 0.1 fusion.77
  99.8 18.3 %collective-permute-done.5 = f32[27,16,128]{2,1,0:T(8,128)S(1)} collective-permute-done((f32[27,16,128]{2,1,0:T(8,128)S(1)}, f32[27,16,128]{2,1,0:T(8,128)S(1)}, u32[]{:S(2)}, u32[]{:S(2)}) %collective-permute-start.5) | collective-permute-done | bytes 221216 | tf_op jit(solution)/shard_map/ppermute | solution.py:16
  118.2 0.1 collective-permute-start.6
  118.3 3.4 %fusion.59 = bf16[1,2,8,16,512]{4,3,2,1,0:T(8,128)(2,1)} fusion(f32[1,2,8,16,512]{4,3,2,1,0:T(8,128)S(1)} %get-tuple-element.26, f32[1,2,8,16,512]{4,3,2,1,0:T(8,128)S(1)} %get-tuple-element.27, f32[1,2,8,16,512]{4,3,2,1,0:T(8,128)S(1)} %get-tuple-element.25, f32[1,2,8,16,512]{4,3,2,1,0:T(8,128)S(1)} %get-tuple-element.41, ...), kind=kLoop, calls=%fused_computation.77 | loop fusion | flops 3538944 | bytes 14417920 | tf_op jit(solution)/shard_map/convert_element_type | solution.py:63
  121.7 6.4 %collective-permute-done.6 = f32[27,16,128]{2,1,0:T(8,128)S(1)} collective-permute-done((f32[27,16,128]{2,1,0:T(8,128)S(1)}, f32[27,16,128]{2,1,0:T(8,128)S(1)}, u32[]{:S(2)}, u32[]{:S(2)}) %collective-permute-start.6) | collective-permute-done | bytes 221216 | tf_op jit(solution)/shard_map/ppermute | solution.py:16
  128.1 0.7 add_multiply_fusion
  (8 shorter events, 0.2 us)
Async XLA Ops:
  7.2 5.0 %copy-start.1 = (bf16[1,2,8,16,512]{4,3,2,1,0:T(8,128)(2,1)S(1)}, bf16[1,2,8,16,512]{4,3,2,1,0:T(8,128)(2,1)}, u32[]{:S(2)}) copy-start(bf16[1,2,8,16,512]{4,3,2,1,0:T(8,128)(2,1)} %param.3) | copy-start | bytes 786436
  7.2 33.5 %all-gather.2.cloned.1.call-start = ((), (), s32[]{:S(2)}) async-start(), calls=%async_computation | async-start | bytes 2359296 | tf_op jit(solution)/shard_map/all_gather | solution.py:35
  9.0 3.7 %copy-start.2 = (bf16[27,16,128]{2,1,0:T(8,128)(2,1)S(1)}, bf16[27,16,128]{2,1,0:T(8,128)(2,1)}, u32[]{:S(2)}) copy-start(bf16[27,16,128]{2,1,0:T(8,128)(2,1)} %param.5) | copy-start | bytes 331780
  40.7 9.0 %copy-start = (bf16[1,2,8,128,512]{4,3,2,1,0:T(8,128)(2,1)S(1)}, bf16[1,2,8,128,512]{4,3,2,1,0:T(8,128)(2,1)}, u32[]{:S(2)}) copy-start(bf16[1,2,8,128,512]{4,3,2,1,0:T(8,128)(2,1)} %all-gather.2.cloned.1.call-done) | copy-start | bytes 6291460
  42.6 28.0 %collective-permute-start = (bf16[1,1,8,128,512]{4,3,2,1,0:T(8,128)(2,1)S(1)}, bf16[1,1,8,128,512]{4,3,2,1,0:T(8,128)(2,1)S(1)}, u32[]{:S(2)}, u32[]{:S(2)}) collective-permute-start(bf16[1,1,8,128,512]{4,3,2,1,0:T(8,128)(2,1)S(1)} %get-tuple-element.3), channel_id=1, source_target_pairs={{16,0},{32,16},{48,32},{64,48},{80,64},{96,80},{112,96},{128,112},... | collective-permute-start | bytes 3145736 | tf_op jit(solution)/shard_map/ppermute | solution.py:11
  47.8 30.6 %collective-permute-start.1 = (bf16[1,1,8,128,512]{4,3,2,1,0:T(8,128)(2,1)S(1)}, bf16[1,1,8,128,512]{4,3,2,1,0:T(8,128)(2,1)S(1)}, u32[]{:S(2)}, u32[]{:S(2)}) collective-permute-start(bf16[1,1,8,128,512]{4,3,2,1,0:T(8,128)(2,1)S(1)} %get-tuple-element.2), channel_id=1, source_target_pairs={{0,16},{16,32},{32,48},{48,64},{64,80},{80,96},{96,112},{112,128},... | collective-permute-start | bytes 3145736 | tf_op jit(solution)/shard_map/ppermute | solution.py:11
  79.2 6.8 %collective-permute-start.2 = (f32[27,16,128]{2,1,0:T(8,128)S(1)}, f32[27,16,128]{2,1,0:T(8,128)S(1)}, u32[]{:S(2)}, u32[]{:S(2)}) collective-permute-start(f32[27,16,128]{2,1,0:T(8,128)S(1)} %bitcast.157), channel_id=1, source_target_pairs={{0,1},{1,0},{2,3},{3,2},{4,5},{5,4},{6,7},{7,6},{8,9},{9,8},{10,11... | collective-permute-start | bytes 663560 | tf_op jit(solution)/shard_map/ppermute | solution.py:16
  86.0 6.0 %collective-permute-start.3 = (f32[27,16,128]{2,1,0:T(8,128)S(1)}, f32[27,16,128]{2,1,0:T(8,128)S(1)}, u32[]{:S(2)}, u32[]{:S(2)}) collective-permute-start(f32[27,16,128]{2,1,0:T(8,128)S(1)} %add.183), channel_id=1, source_target_pairs={{0,16},{16,0},{32,48},{48,32},{64,80},{80,64},{96,112},{112,96},{1... | collective-permute-start | bytes 663560 | tf_op jit(solution)/shard_map/ppermute | solution.py:16
  92.1 7.5 %collective-permute-start.4 = (f32[27,16,128]{2,1,0:T(8,128)S(1)}, f32[27,16,128]{2,1,0:T(8,128)S(1)}, u32[]{:S(2)}, u32[]{:S(2)}) collective-permute-start(f32[27,16,128]{2,1,0:T(8,128)S(1)} %add.184), channel_id=1, source_target_pairs={{0,128},{16,144},{32,160},{48,176},{64,192},{80,208},{96,224},{112... | collective-permute-start | bytes 663560 | tf_op jit(solution)/shard_map/ppermute | solution.py:16
  99.6 18.6 %collective-permute-start.5 = (f32[27,16,128]{2,1,0:T(8,128)S(1)}, f32[27,16,128]{2,1,0:T(8,128)S(1)}, u32[]{:S(2)}, u32[]{:S(2)}) collective-permute-start(f32[27,16,128]{2,1,0:T(8,128)S(1)} %add.185), channel_id=1, source_target_pairs={{0,32},{16,48},{32,0},{48,16},{64,96},{80,112},{96,64},{112,80},{1... | collective-permute-start | bytes 663560 | tf_op jit(solution)/shard_map/ppermute | solution.py:16
  118.2 9.9 %collective-permute-start.6 = (f32[27,16,128]{2,1,0:T(8,128)S(1)}, f32[27,16,128]{2,1,0:T(8,128)S(1)}, u32[]{:S(2)}, u32[]{:S(2)}) collective-permute-start(f32[27,16,128]{2,1,0:T(8,128)S(1)} %add.186), channel_id=1, source_target_pairs={{0,64},{16,80},{32,96},{48,112},{64,0},{80,16},{96,32},{112,48},{1... | collective-permute-start | bytes 663560 | tf_op jit(solution)/shard_map/ppermute | solution.py:16
Sparse Core Ops, SparseCore 0:
  9.8 30.7 all-gather.1
where the time goes:
time: 136 us
  waiting for transfers between devices  93.1 us (68%)
  between operations  14.3 us (11%)
  starting transfers between devices  9.7 us (7%)
  local copies, waits for them, and re-layouts  8.23 us (6%)
  matrix products  6.09 us (4%)
  other arithmetic  4.23 us (3%)
    ppermute x5, waiting for transfers between devices, exchange_sum(): lax.ppermute(value, axis, [(i, i ^ distance) for i in range(count)])  39.2 us
    all_gather x1, waiting for transfers between devices, local(): gathered = lax.all_gather(cotangent, 'chan', axis=3, tiled=True)  28 us
    ppermute x2, waiting for transfers between devices, from_behind(): lax.ppermute(value, axis, [(source, source + steps) for source in range(i...  25.3 us
    ppermute x2, starting transfers between devices, from_behind(): lax.ppermute(value, axis, [(source, source + steps) for source in range(i...  7.13 us
    unnamed x14, local copies, waits for them, and re-layouts  4.55 us
    dot_general x9, matrix products, local(): jnp.einsum('bxzcy,kc->bxzky', slab, kernel, preferred_element_type=jnp.fl...  3.78 us
    convert_element_type x1, other arithmetic, local(): input_grad = accum.astype(jnp.bfloat16)  3.38 us
  transfers between devices with their start and end apart: 8, of which 8 were waited for; matrix products, arithmetic and copies ran while one was open for 11% of the time, Pallas kernels for 0%

commit v1 on v0

--- a/solution.py
+++ b/solution.py
@@ -3,6 +3,15 @@
 import jax.numpy as jnp
 from jax import lax
 from jax.sharding import PartitionSpec as P
+from jax.lax import axis_index, axis_size, ppermute
+
+
+def rest_files_in(xx, array_dim):
+    xx = jnp.moveaxis(xx, 0, array_dim)
+    back = xx.shape
+    return xx.reshape(
+        *back[:array_dim], back[array_dim] * back[array_dim + 1], *back[array_dim + 2 :]
+    )
 
 
 def from_behind(value, axis, steps):
@@ -32,7 +41,23 @@
 def local(inputs, cotangent, weight):
     samples, planes, depth, channels, width = inputs.shape
     outputs = weight.shape[2]
-    gathered = lax.all_gather(cotangent, "chan", axis=3, tiled=True)
+    n_shards = axis_size("chan")
+    buffer = [(b, (b + 1) % n_shards) for b in range(n_shards)]
+    stack_in = [(rr, i0) for i0, rr in buffer]
+    reached, built = ([], [])
+    for u in range(n_shards - 1):
+        if u % 2 == 0:
+            t_next = ppermute(reached[-1] if reached else cotangent, axis_name="chan", perm=buffer)
+            reached.append(t_next)
+        else:
+            built.append(
+                ppermute(built[-1] if built else cotangent, axis_name="chan", perm=stack_in)
+            )
+    f_next = jnp.stack([*reached[::-1], cotangent, *built], axis=0)
+    main = axis_index("chan")
+    p_next = main - len(reached)
+    f_next = f_next[(jnp.arange(n_shards) - p_next) % n_shards]
+    gathered = rest_files_in(f_next, 3)
     lower_plane = from_behind(gathered[:, -1:], "space", 1)
     upper_plane = from_behind(gathered[:, :1], "space", -1)
     stacked = jnp.concatenate(

time: 136 us -> 119 us (0.88)
  the two profiles are of different devices: /device:TPU:4 before, /device:TPU:25 now
where the time goes in v1:
time: 119 us; the launch traced here: 118 us
  waiting for transfers between devices  59.4 us (50%)
  starting transfers between devices  29.7 us (25%)
  local copies, waits for them, and re-layouts  17.5 us (15%)
  matrix products  6.07 us (5%)
  other arithmetic  4.77 us (4%)
    ppermute x5, waiting for transfers between devices, exchange_sum(): lax.ppermute(value, axis, [(i, i ^ distance) for i in range(count)])  31.2 us
    ppermute x2, waiting for transfers between devices, from_behind(): lax.ppermute(value, axis, [(source, source + steps) for source in range(i...  20 us
    ppermute x5, starting transfers between devices, exchange_sum(): lax.ppermute(value, axis, [(i, i ^ distance) for i in range(count)])  13.9 us
    ppermute x4, starting transfers between devices, local(): ppermute(reached[-1] if reached else cotangent, axis_name='chan', perm=bu...  12.6 us
    unnamed x37, local copies, waits for them, and re-layouts  11.8 us
    ppermute x4, waiting for transfers between devices, local(): ppermute(reached[-1] if reached else cotangent, axis_name='chan', perm=bu...  8.17 us
    dot_general x9, matrix products, local(): jnp.einsum('bxzcy,kc->bxzky', slab, kernel, preferred_element_type=jnp.fl...  3.77 us
    convert_element_type x1, other arithmetic, local(): input_grad = accum.astype(jnp.bfloat16)  3.32 us
  transfers between devices with their start and end apart: 14, of which 10 were waited for; matrix products, arithmetic and copies ran while one was open for 18% of the time, Pallas kernels for 0%

profile of v1, /device:TPU:25, one launch (start us, length us, event | category | flops | bytes accessed | tf_op | source)
XLA Modules:
  0.0 118.5 jit_solution(1809904890247411965)
XLA Ops:
  0.6 2.2 %collective-permute-start = (bf16[1,2,8,16,512]{4,3,2,1,0:T(8,128)(2,1)}, bf16[1,2,8,16,512]{4,3,2,1,0:T(8,128)(2,1)S(1)}, u32[]{:S(2)}, u32[]{:S(2)}) collective-permute-start(bf16[1,2,8,16,512]{4,3,2,1,0:T(8,128)(2,1)} %param.4), channel_id=1, source_target_pairs={{0,2},{2,4},{4,6},{6,8},{8,10},{10,12},{12,14},{14,0},{1,3},{3,5},... | collective-permute-start | bytes 786440 | tf_op jit(solution)/shard_map/ppermute | solution.py:50
  2.9 1.1 fusion.46
  4.0 1.0 fusion.42
  5.0 1.1 fusion.47
  6.0 1.1 fusion.44
  7.1 3.0 %collective-permute-start.1 = (bf16[1,2,8,16,512]{4,3,2,1,0:T(8,128)(2,1)S(1)}, bf16[1,2,8,16,512]{4,3,2,1,0:T(8,128)(2,1)S(1)}, u32[]{:S(2)}, u32[]{:S(2)}) collective-permute-start(bf16[1,2,8,16,512]{4,3,2,1,0:T(8,128)(2,1)S(1)} %collective-permute-done), channel_id=1, source_target_pairs={{0,2},{2,4},{4,6},{6,8},{8,10},{10,12},{12,14},{14,0},{1,3},{3,5},... | collective-permute-start | bytes 786440 | tf_op jit(solution)/shard_map/ppermute | solution.py:50
  10.1 0.1 fusion.45
  10.3 0.1 fusion.48
  10.4 3.0 %collective-permute-done.1 = bf16[1,2,8,16,512]{4,3,2,1,0:T(8,128)(2,1)S(1)} collective-permute-done((bf16[1,2,8,16,512]{4,3,2,1,0:T(8,128)(2,1)S(1)}, bf16[1,2,8,16,512]{4,3,2,1,0:T(8,128)(2,1)S(1)}, u32[]{:S(2)}, u32[]{:S(2)}) %collective-permute-start.1) | collective-permute-done | bytes 262176 | tf_op jit(solution)/shard_map/ppermute | solution.py:50
  13.4 3.7 %collective-permute-start.2 = (bf16[1,2,8,16,512]{4,3,2,1,0:T(8,128)(2,1)S(1)}, bf16[1,2,8,16,512]{4,3,2,1,0:T(8,128)(2,1)S(1)}, u32[]{:S(2)}, u32[]{:S(2)}) collective-permute-start(bf16[1,2,8,16,512]{4,3,2,1,0:T(8,128)(2,1)S(1)} %collective-permute-done.1), channel_id=1, source_target_pairs={{0,2},{2,4},{4,6},{6,8},{8,10},{10,12},{12,14},{14,0},{1,3},{3,5},... | collective-permute-start | bytes 786440 | tf_op jit(solution)/shard_map/ppermute | solution.py:50
  17.2 0.1 fusion.49
  17.3 3.1 %collective-permute-done.2 = bf16[1,2,8,16,512]{4,3,2,1,0:T(8,128)(2,1)S(1)} collective-permute-done((bf16[1,2,8,16,512]{4,3,2,1,0:T(8,128)(2,1)S(1)}, bf16[1,2,8,16,512]{4,3,2,1,0:T(8,128)(2,1)S(1)}, u32[]{:S(2)}, u32[]{:S(2)}) %collective-permute-start.2) | collective-permute-done | bytes 262176 | tf_op jit(solution)/shard_map/ppermute | solution.py:50
  20.4 3.7 %collective-permute-start.3 = (bf16[1,2,8,16,512]{4,3,2,1,0:T(8,128)(2,1)S(1)}, bf16[1,2,8,16,512]{4,3,2,1,0:T(8,128)(2,1)S(1)}, u32[]{:S(2)}, u32[]{:S(2)}) collective-permute-start(bf16[1,2,8,16,512]{4,3,2,1,0:T(8,128)(2,1)S(1)} %collective-permute-done.2), channel_id=1, source_target_pairs={{0,2},{2,4},{4,6},{6,8},{8,10},{10,12},{12,14},{14,0},{1,3},{3,5},... | collective-permute-start | bytes 786440 | tf_op jit(solution)/shard_map/ppermute | solution.py:50
  24.1 0.6 pad_clamp_fusion
  24.7 0.6 fusion.62
  25.4 2.1 %collective-permute-done.3 = bf16[1,2,8,16,512]{4,3,2,1,0:T(8,128)(2,1)S(1)} collective-permute-done((bf16[1,2,8,16,512]{4,3,2,1,0:T(8,128)(2,1)S(1)}, bf16[1,2,8,16,512]{4,3,2,1,0:T(8,128)(2,1)S(1)}, u32[]{:S(2)}, u32[]{:S(2)}) %collective-permute-start.3) | collective-permute-done | bytes 262176 | tf_op jit(solution)/shard_map/ppermute | solution.py:50
  27.4 0.7 bitcast_dynamic-update-slice_fusion.4
  28.2 0.7 bitcast_dynamic-update-slice_fusion.3
  28.9 0.7 bitcast_dynamic-update-slice_fusion.2
  29.6 0.7 bitcast_dynamic-update-slice_fusion.7
  30.4 0.7 bitcast_dynamic-update-slice_fusion.6
  31.1 0.7 bitcast_dynamic-update-slice_fusion.1
  31.8 0.7 bitcast_dynamic-update-slice_fusion
  32.5 0.7 bitcast_dynamic-update-slice_fusion.5
  33.2 2.4 %gather_fusion = bf16[8,2,8,16,512]{4,3,2,1,0:T(8,128)(2,1)S(1)} fusion(bf16[8,2,8,16,512]{4,3,2,1,0:T(8,128)(2,1)} %bitcast.13, s32[1024]{0:T(1024)} %pad_clamp_fusion), kind=kCustom, calls=%fused_computation | custom fusion | bytes 4194336 | tf_op jit(solution)/shard_map/gather | solution.py:59
  35.6 0.2 copy.11
  35.9 0.2 fusion.52
  36.1 1.9 %collective-permute-start.8 = (bf16[1,1,8,128,512]{4,3,2,1,0:T(8,128)(2,1)S(1)}, bf16[1,1,8,128,512]{4,3,2,1,0:T(8,128)(2,1)S(1)}, u32[]{:S(2)}, u32[]{:S(2)}) collective-permute-start(bf16[1,1,8,128,512]{4,3,2,1,0:T(8,128)(2,1)S(1)} %get-tuple-element.2), channel_id=1, source_target_pairs={{0,16},{16,32},{32,48},{48,64},{64,80},{80,96},{96,112},{112,128},... | collective-permute-start | bytes 3145736 | tf_op jit(solution)/shard_map/ppermute | solution.py:20
  38.0 1.3 %collective-permute-start.7 = (bf16[1,1,8,128,512]{4,3,2,1,0:T(8,128)(2,1)S(1)}, bf16[1,1,8,128,512]{4,3,2,1,0:T(8,128)(2,1)S(1)}, u32[]{:S(2)}, u32[]{:S(2)}) collective-permute-start(bf16[1,1,8,128,512]{4,3,2,1,0:T(8,128)(2,1)S(1)} %get-tuple-element.3), channel_id=1, source_target_pairs={{16,0},{32,16},{48,32},{64,48},{80,64},{96,80},{112,96},{128,112},... | collective-permute-start | bytes 3145736 | tf_op jit(solution)/shard_map/ppermute | solution.py:20
  39.3 0.4 convolution_bitcast_fusion.3
  39.7 0.1 fusion.58
  39.9 0.6 copy-done.9
  40.4 0.4 convolution_bitcast_fusion.4
  40.9 0.4 convolution_bitcast_fusion.5
  41.3 0.4 fusion.56
  41.7 1.2 %copy-done.2 = bf16[1,2,8,144,512]{4,3,2,1,0:T(8,128)(2,1)S(1)} copy-done((bf16[1,2,8,144,512]{4,3,2,1,0:T(8,128)(2,1)S(1)}, bf16[1,2,8,144,512]{4,3,2,1,0:T(8,128)(2,1)}, u32[]{:S(2)}) %copy-start.2) | copy-done | bytes 2359320
  42.9 0.8 fusion.9
  43.7 16.6 %collective-permute-done.8 = bf16[1,1,8,128,512]{4,3,2,1,0:T(8,128)(2,1)S(1)} collective-permute-done((bf16[1,1,8,128,512]{4,3,2,1,0:T(8,128)(2,1)S(1)}, bf16[1,1,8,128,512]{4,3,2,1,0:T(8,128)(2,1)S(1)}, u32[]{:S(2)}, u32[]{:S(2)}) %collective-permute-start.8) | collective-permute-done | bytes 1048608 | tf_op jit(solution)/shard_map/ppermute | solution.py:20
  60.3 0.8 fusion.12
  61.1 3.4 %collective-permute-done.7 = bf16[1,1,8,128,512]{4,3,2,1,0:T(8,128)(2,1)S(1)} collective-permute-done((bf16[1,1,8,128,512]{4,3,2,1,0:T(8,128)(2,1)S(1)}, bf16[1,1,8,128,512]{4,3,2,1,0:T(8,128)(2,1)S(1)}, u32[]{:S(2)}, u32[]{:S(2)}) %collective-permute-start.7) | collective-permute-done | bytes 1048608 | tf_op jit(solution)/shard_map/ppermute | solution.py:20
  64.5 0.8 fusion.6
  65.3 1.3 %collective-permute-start.9 = (f32[27,16,128]{2,1,0:T(8,128)S(1)}, f32[27,16,128]{2,1,0:T(8,128)S(1)}, u32[]{:S(2)}, u32[]{:S(2)}) collective-permute-start(f32[27,16,128]{2,1,0:T(8,128)S(1)} %bitcast.190), channel_id=1, source_target_pairs={{0,1},{1,0},{2,3},{3,2},{4,5},{5,4},{6,7},{7,6},{8,9},{9,8},{10,11... | collective-permute-start | bytes 663560 | tf_op jit(solution)/shard_map/ppermute | solution.py:25
  66.6 0.4 convolution_bitcast_fusion.7
  67.0 0.4 convolution_bitcast_fusion.8
  67.5 0.3 fusion.53
  67.8 0.4 copy-done.5
  68.2 0.4 convolution_bitcast_fusion.1
  68.6 0.4 convolution_bitcast_fusion.2
  69.0 3.0 %collective-permute-done.9 = f32[27,16,128]{2,1,0:T(8,128)S(1)} collective-permute-done((f32[27,16,128]{2,1,0:T(8,128)S(1)}, f32[27,16,128]{2,1,0:T(8,128)S(1)}, u32[]{:S(2)}, u32[]{:S(2)}) %collective-permute-start.9) | collective-permute-done | bytes 221216 | tf_op jit(solution)/shard_map/ppermute | solution.py:25
  72.1 1.7 %collective-permute-start.10 = (f32[27,16,128]{2,1,0:T(8,128)S(1)}, f32[27,16,128]{2,1,0:T(8,128)S(1)}, u32[]{:S(2)}, u32[]{:S(2)}) collective-permute-start(f32[27,16,128]{2,1,0:T(8,128)S(1)} %add.209), channel_id=1, source_target_pairs={{0,16},{16,0},{32,48},{48,32},{64,80},{80,64},{96,112},{112,96},{1... | collective-permute-start | bytes 663560 | tf_op jit(solution)/shard_map/ppermute | solution.py:25
  73.8 0.3 fusion.59
  74.1 0.4 convolution_bitcast_fusion.6
  74.6 3.8 %collective-permute-done.10 = f32[27,16,128]{2,1,0:T(8,128)S(1)} collective-permute-done((f32[27,16,128]{2,1,0:T(8,128)S(1)}, f32[27,16,128]{2,1,0:T(8,128)S(1)}, u32[]{:S(2)}, u32[]{:S(2)}) %collective-permute-start.10) | collective-permute-done | bytes 221216 | tf_op jit(solution)/shard_map/ppermute | solution.py:25
  78.4 6.0 %collective-permute-start.11 = (f32[27,16,128]{2,1,0:T(8,128)S(1)}, f32[27,16,128]{2,1,0:T(8,128)S(1)}, u32[]{:S(2)}, u32[]{:S(2)}) collective-permute-start(f32[27,16,128]{2,1,0:T(8,128)S(1)} %add.210), channel_id=1, source_target_pairs={{0,128},{16,144},{32,160},{48,176},{64,192},{80,208},{96,224},{112... | collective-permute-start | bytes 663560 | tf_op jit(solution)/shard_map/ppermute | solution.py:25
  84.3 0.1 fusion.55
  84.5 0.4 convolution_bitcast_fusion
  84.9 3.9 %collective-permute-done.11 = f32[27,16,128]{2,1,0:T(8,128)S(1)} collective-permute-done((f32[27,16,128]{2,1,0:T(8,128)S(1)}, f32[27,16,128]{2,1,0:T(8,128)S(1)}, u32[]{:S(2)}, u32[]{:S(2)}) %collective-permute-start.11) | collective-permute-done | bytes 221216 | tf_op jit(solution)/shard_map/ppermute | solution.py:25
  88.9 1.8 %collective-permute-start.12 = (f32[27,16,128]{2,1,0:T(8,128)S(1)}, f32[27,16,128]{2,1,0:T(8,128)S(1)}, u32[]{:S(2)}, u32[]{:S(2)}) collective-permute-start(f32[27,16,128]{2,1,0:T(8,128)S(1)} %add.211), channel_id=1, source_target_pairs={{0,32},{16,48},{32,0},{48,16},{64,96},{80,112},{96,64},{112,80},{1... | collective-permute-start | bytes 663560 | tf_op jit(solution)/shard_map/ppermute | solution.py:25
  90.6 0.1 fusion.61
  90.8 10.9 %collective-permute-done.12 = f32[27,16,128]{2,1,0:T(8,128)S(1)} collective-permute-done((f32[27,16,128]{2,1,0:T(8,128)S(1)}, f32[27,16,128]{2,1,0:T(8,128)S(1)}, u32[]{:S(2)}, u32[]{:S(2)}) %collective-permute-start.12) | collective-permute-done | bytes 221216 | tf_op jit(solution)/shard_map/ppermute | solution.py:25
  101.7 3.2 %collective-permute-start.13 = (f32[27,16,128]{2,1,0:T(8,128)S(1)}, f32[27,16,128]{2,1,0:T(8,128)S(1)}, u32[]{:S(2)}, u32[]{:S(2)}) collective-permute-start(f32[27,16,128]{2,1,0:T(8,128)S(1)} %add.212), channel_id=1, source_target_pairs={{0,64},{16,80},{32,96},{48,112},{64,0},{80,16},{96,32},{112,48},{1... | collective-permute-start | bytes 663560 | tf_op jit(solution)/shard_map/ppermute | solution.py:25
  104.9 3.3 %fusion.41 = bf16[1,2,8,16,512]{4,3,2,1,0:T(8,128)(2,1)} fusion(f32[1,2,8,16,512]{4,3,2,1,0:T(8,128)S(1)} %get-tuple-element.26, f32[1,2,8,16,512]{4,3,2,1,0:T(8,128)S(1)} %get-tuple-element.27, f32[1,2,8,16,512]{4,3,2,1,0:T(8,128)S(1)} %get-tuple-element.25, f32[1,2,8,16,512]{4,3,2,1,0:T(8,128)S(1)} %get-tuple-element.41, ...), kind=kLoop, calls=%fused_computation.71 | loop fusion | flops 3538944 | bytes 14417920 | tf_op jit(solution)/shard_map/convert_element_type | solution.py:88
  108.2 9.6 %collective-permute-done.13 = f32[27,16,128]{2,1,0:T(8,128)S(1)} collective-permute-done((f32[27,16,128]{2,1,0:T(8,128)S(1)}, f32[27,16,128]{2,1,0:T(8,128)S(1)}, u32[]{:S(2)}, u32[]{:S(2)}) %collective-permute-start.13) | collective-permute-done | bytes 221216 | tf_op jit(solution)/shard_map/ppermute | solution.py:25
  117.8 0.7 add_multiply_fusion
  (34 shorter events, 0.3 us)
Async XLA Ops:
  0.6 9.5 %copy-start = (bf16[1,2,8,16,512]{4,3,2,1,0:T(8,128)(2,1)S(1)}, bf16[1,2,8,16,512]{4,3,2,1,0:T(8,128)(2,1)}, u32[]{:S(2)}) copy-start(bf16[1,2,8,16,512]{4,3,2,1,0:T(8,128)(2,1)} %param.3) | copy-start | bytes 786436
  0.6 6.5 %collective-permute-start = (bf16[1,2,8,16,512]{4,3,2,1,0:T(8,128)(2,1)}, bf16[1,2,8,16,512]{4,3,2,1,0:T(8,128)(2,1)S(1)}, u32[]{:S(2)}, u32[]{:S(2)}) collective-permute-start(bf16[1,2,8,16,512]{4,3,2,1,0:T(8,128)(2,1)} %param.4), channel_id=1, source_target_pairs={{0,2},{2,4},{4,6},{6,8},{8,10},{10,12},{12,14},{14,0},{1,3},{3,5},... | collective-permute-start | bytes 786440 | tf_op jit(solution)/shard_map/ppermute | solution.py:50
  2.9 14.4 %collective-permute-start.4 = (bf16[1,2,8,16,512]{4,3,2,1,0:T(8,128)(2,1)}, bf16[1,2,8,16,512]{4,3,2,1,0:T(8,128)(2,1)S(1)}, u32[]{:S(2)}, u32[]{:S(2)}) collective-permute-start(bf16[1,2,8,16,512]{4,3,2,1,0:T(8,128)(2,1)} %param.4), channel_id=1, source_target_pairs={{2,0},{4,2},{6,4},{8,6},{10,8},{12,10},{14,12},{0,14},{3,1},{5,3},... | collective-permute-start | bytes 786440 | tf_op jit(solution)/shard_map/ppermute | solution.py:54
  3.9 20.8 %copy-start.4 = (bf16[27,16,128]{2,1,0:T(8,128)(2,1)S(1)}, bf16[27,16,128]{2,1,0:T(8,128)(2,1)}, u32[]{:S(2)}) copy-start(bf16[27,16,128]{2,1,0:T(8,128)(2,1)} %param.5) | copy-start | bytes 331780
  7.1 6.3 %collective-permute-start.1 = (bf16[1,2,8,16,512]{4,3,2,1,0:T(8,128)(2,1)S(1)}, bf16[1,2,8,16,512]{4,3,2,1,0:T(8,128)(2,1)S(1)}, u32[]{:S(2)}, u32[]{:S(2)}) collective-permute-start(bf16[1,2,8,16,512]{4,3,2,1,0:T(8,128)(2,1)S(1)} %collective-permute-done), channel_id=1, source_target_pairs={{0,2},{2,4},{4,6},{6,8},{8,10},{10,12},{12,14},{14,0},{1,3},{3,5},... | collective-permute-start | bytes 786440 | tf_op jit(solution)/shard_map/ppermute | solution.py:50
  10.1 20.2 %copy-start.3 = (bf16[1,2,8,16,512]{4,3,2,1,0:T(8,128)(2,1)S(1)}, bf16[1,2,8,16,512]{4,3,2,1,0:T(8,128)(2,1)}, u32[]{:S(2)}) copy-start(bf16[1,2,8,16,512]{4,3,2,1,0:T(8,128)(2,1)} %param.4) | copy-start | bytes 786436
  13.4 7.0 %collective-permute-start.2 = (bf16[1,2,8,16,512]{4,3,2,1,0:T(8,128)(2,1)S(1)}, bf16[1,2,8,16,512]{4,3,2,1,0:T(8,128)(2,1)S(1)}, u32[]{:S(2)}, u32[]{:S(2)}) collective-permute-start(bf16[1,2,8,16,512]{4,3,2,1,0:T(8,128)(2,1)S(1)} %collective-permute-done.1), channel_id=1, source_target_pairs={{0,2},{2,4},{4,6},{6,8},{8,10},{10,12},{12,14},{14,0},{1,3},{3,5},... | collective-permute-start | bytes 786440 | tf_op jit(solution)/shard_map/ppermute | solution.py:50
  17.3 15.9 %copy-start.1 = (bf16[1,2,8,144,512]{4,3,2,1,0:T(8,128)(2,1)}, bf16[1,2,8,144,512]{4,3,2,1,0:T(8,128)(2,1)S(1)}, u32[]{:S(2)}) copy-start(bf16[1,2,8,144,512]{4,3,2,1,0:T(8,128)(2,1)S(1)} %fusion.49) | copy-start | bytes 7077892
  17.3 8.0 %collective-permute-start.5 = (bf16[1,2,8,16,512]{4,3,2,1,0:T(8,128)(2,1)S(1)}, bf16[1,2,8,16,512]{4,3,2,1,0:T(8,128)(2,1)S(1)}, u32[]{:S(2)}, u32[]{:S(2)}) collective-permute-start(bf16[1,2,8,16,512]{4,3,2,1,0:T(8,128)(2,1)S(1)} %collective-permute-done.4), channel_id=1, source_target_pairs={{2,0},{4,2},{6,4},{8,6},{10,8},{12,10},{14,12},{0,14},{3,1},{5,3},... | collective-permute-start | bytes 786440 | tf_op jit(solution)/shard_map/ppermute | solution.py:54
  20.4 7.0 %collective-permute-start.3 = (bf16[1,2,8,16,512]{4,3,2,1,0:T(8,128)(2,1)S(1)}, bf16[1,2,8,16,512]{4,3,2,1,0:T(8,128)(2,1)S(1)}, u32[]{:S(2)}, u32[]{:S(2)}) collective-permute-start(bf16[1,2,8,16,512]{4,3,2,1,0:T(8,128)(2,1)S(1)} %collective-permute-done.2), channel_id=1, source_target_pairs={{0,2},{2,4},{4,6},{6,8},{8,10},{10,12},{12,14},{14,0},{1,3},{3,5},... | collective-permute-start | bytes 786440 | tf_op jit(solution)/shard_map/ppermute | solution.py:50
  25.3 7.2 %collective-permute-start.6 = (bf16[1,2,8,16,512]{4,3,2,1,0:T(8,128)(2,1)S(1)}, bf16[1,2,8,16,512]{4,3,2,1,0:T(8,128)(2,1)S(1)}, u32[]{:S(2)}, u32[]{:S(2)}) collective-permute-start(bf16[1,2,8,16,512]{4,3,2,1,0:T(8,128)(2,1)S(1)} %collective-permute-done.5), channel_id=1, source_target_pairs={{2,0},{4,2},{6,4},{8,6},{10,8},{12,10},{14,12},{0,14},{3,1},{5,3},... | collective-permute-start | bytes 786440 | tf_op jit(solution)/shard_map/ppermute | solution.py:54
  35.8 3.4 %copy-start.10 = (bf16[3,16,128]{2,1,0:T(8,128)(2,1)S(1)}, bf16[3,16,128]{2,1,0:T(8,128)(2,1)}, u32[]{:S(2)}) copy-start(bf16[3,16,128]{2,1,0:T(8,128)(2,1)} %get-tuple-element.30) | copy-start | bytes 36868
  36.1 24.3 %collective-permute-start.8 = (bf16[1,1,8,128,512]{4,3,2,1,0:T(8,128)(2,1)S(1)}, bf16[1,1,8,128,512]{4,3,2,1,0:T(8,128)(2,1)S(1)}, u32[]{:S(2)}, u32[]{:S(2)}) collective-permute-start(bf16[1,1,8,128,512]{4,3,2,1,0:T(8,128)(2,1)S(1)} %get-tuple-element.2), channel_id=1, source_target_pairs={{0,16},{16,32},{32,48},{48,64},{64,80},{80,96},{96,112},{112,128},... | collective-permute-start | bytes 3145736 | tf_op jit(solution)/shard_map/ppermute | solution.py:20
  38.0 26.5 %collective-permute-start.7 = (bf16[1,1,8,128,512]{4,3,2,1,0:T(8,128)(2,1)S(1)}, bf16[1,1,8,128,512]{4,3,2,1,0:T(8,128)(2,1)S(1)}, u32[]{:S(2)}, u32[]{:S(2)}) collective-permute-start(bf16[1,1,8,128,512]{4,3,2,1,0:T(8,128)(2,1)S(1)} %get-tuple-element.3), channel_id=1, source_target_pairs={{16,0},{32,16},{48,32},{64,48},{80,64},{96,80},{112,96},{128,112},... | collective-permute-start | bytes 3145736 | tf_op jit(solution)/shard_map/ppermute | solution.py:20
  39.7 0.7 copy-start.9
  39.8 1.0 copy-start.8
  41.3 1.7 %copy-start.2 = (bf16[1,2,8,144,512]{4,3,2,1,0:T(8,128)(2,1)S(1)}, bf16[1,2,8,144,512]{4,3,2,1,0:T(8,128)(2,1)}, u32[]{:S(2)}) copy-start(bf16[1,2,8,144,512]{4,3,2,1,0:T(8,128)(2,1)} %copy-done.1) | copy-start | bytes 7077892
  61.1 5.5 %copy-start.7 = (bf16[3,16,128]{2,1,0:T(8,128)(2,1)S(1)}, bf16[3,16,128]{2,1,0:T(8,128)(2,1)}, u32[]{:S(2)}) copy-start(bf16[3,16,128]{2,1,0:T(8,128)(2,1)} %get-tuple-element.34) | copy-start | bytes 36868
  65.3 1.8 %copy-start.6 = (bf16[3,16,128]{2,1,0:T(8,128)(2,1)S(1)}, bf16[3,16,128]{2,1,0:T(8,128)(2,1)}, u32[]{:S(2)}) copy-start(bf16[3,16,128]{2,1,0:T(8,128)(2,1)} %get-tuple-element.28) | copy-start | bytes 36868
  65.3 6.7 %collective-permute-start.9 = (f32[27,16,128]{2,1,0:T(8,128)S(1)}, f32[27,16,128]{2,1,0:T(8,128)S(1)}, u32[]{:S(2)}, u32[]{:S(2)}) collective-permute-start(f32[27,16,128]{2,1,0:T(8,128)S(1)} %bitcast.190), channel_id=1, source_target_pairs={{0,1},{1,0},{2,3},{3,2},{4,5},{5,4},{6,7},{7,6},{8,9},{9,8},{10,11... | collective-permute-start | bytes 663560 | tf_op jit(solution)/shard_map/ppermute | solution.py:25
  67.5 0.7 copy-start.5
  72.1 6.2 %collective-permute-start.10 = (f32[27,16,128]{2,1,0:T(8,128)S(1)}, f32[27,16,128]{2,1,0:T(8,128)S(1)}, u32[]{:S(2)}, u32[]{:S(2)}) collective-permute-start(f32[27,16,128]{2,1,0:T(8,128)S(1)} %add.209), channel_id=1, source_target_pairs={{0,16},{16,0},{32,48},{48,32},{64,80},{80,64},{96,112},{112,96},{1... | collective-permute-start | bytes 663560 | tf_op jit(solution)/shard_map/ppermute | solution.py:25
  78.4 10.5 %collective-permute-start.11 = (f32[27,16,128]{2,1,0:T(8,128)S(1)}, f32[27,16,128]{2,1,0:T(8,128)S(1)}, u32[]{:S(2)}, u32[]{:S(2)}) collective-permute-start(f32[27,16,128]{2,1,0:T(8,128)S(1)} %add.210), channel_id=1, source_target_pairs={{0,128},{16,144},{32,160},{48,176},{64,192},{80,208},{96,224},{112... | collective-permute-start | bytes 663560 | tf_op jit(solution)/shard_map/ppermute | solution.py:25
  88.9 12.8 %collective-permute-start.12 = (f32[27,16,128]{2,1,0:T(8,128)S(1)}, f32[27,16,128]{2,1,0:T(8,128)S(1)}, u32[]{:S(2)}, u32[]{:S(2)}) collective-permute-start(f32[27,16,128]{2,1,0:T(8,128)S(1)} %add.211), channel_id=1, source_target_pairs={{0,32},{16,48},{32,0},{48,16},{64,96},{80,112},{96,64},{112,80},{1... | collective-permute-start | bytes 663560 | tf_op jit(solution)/shard_map/ppermute | solution.py:25
  101.7 16.1 %collective-permute-start.13 = (f32[27,16,128]{2,1,0:T(8,128)S(1)}, f32[27,16,128]{2,1,0:T(8,128)S(1)}, u32[]{:S(2)}, u32[]{:S(2)}) collective-permute-start(f32[27,16,128]{2,1,0:T(8,128)S(1)} %add.212), channel_id=1, source_target_pairs={{0,64},{16,80},{32,96},{48,112},{64,0},{80,16},{96,32},{112,48},{1... | collective-permute-start | bytes 663560 | tf_op jit(solution)/shard_map/ppermute | solution.py:25
